TPU v7x, 768 devices: a whole 4x8x12 slice. The times are simulated.
768 devices in a mesh: row: 32 (over x, y_lo, core), col: 24 (over y_hi, z).
Axes of the slice: x: 4, y: 8 (y_hi: 2, y_lo: 4; y = y_hi * 4 + y_lo), z: 12, core: 2. Of those that a mesh axis runs over, the one named last changes fastest.
Arguments:
- inputs: bfloat16 [1536, 8192], P(None, 'row'), may hold values from -6 to 6
- gate_weight: bfloat16 [8192, 27648], P('row', 'col'), may hold values from -0.0625 to 0.0625
- up_weight: bfloat16 [8192, 27648], P('row', 'col'), may hold values from -0.0625 to 0.0625
- gate_pre: bfloat16 [1536, 27648], P('row', 'col'), may hold values from -6 to 6
- up_pre: bfloat16 [1536, 27648], P('row', 'col'), may hold values from -6 to 6
- grad_act: bfloat16 [1536, 27648], P('row', 'col'), may hold values from -1.1953125 to 1.1953125
Outputs:
- grad_input: bfloat16 [1536, 8192], P('col', 'row')
- grad_gate_weight: bfloat16 [8192, 27648], P('row', 'col')
- grad_up_weight: bfloat16 [8192, 27648], P('row', 'col')
All inputs are finite; a program needn't handle non-finite values.
Results may differ from a plain program's by a relative error of at most 0.0049.
Values may be sent and summed in bfloat16 or wider, within the bound.
No kernel may reach another device: no remote copies, remote signals or barrier semaphores. Data moves between devices by JAX's collectives and lax.ppermute only.
A program may use at most 32 MiB of HBM per device.

v0:
```python
import jax
import jax.numpy as jnp
from jax import lax
from jax.sharding import PartitionSpec as P


def contract_rows(left, right):
    return lax.dot_general(
        left, right, (((0,), (0,)), ((), ())), preferred_element_type=jnp.float32
    )


def contract_cols(left, right):
    return lax.dot_general(
        left, right, (((1,), (1,)), ((), ())), preferred_element_type=jnp.float32
    )


def reduce_input(partial_input):
    return lax.psum_scatter(partial_input, "col", scatter_dimension=0, tiled=True).astype(
        jnp.bfloat16
    )


def on_device(inputs, gate_weight, up_weight, gate_pre, up_pre, grad_act):
    gate32 = gate_pre.astype(jnp.float32)
    up32 = up_pre.astype(jnp.float32)
    grad32 = grad_act.astype(jnp.float32)
    sig = jax.nn.sigmoid(gate32)
    grad_gate = (grad32 * up32 * sig * (1.0 + gate32 * (1.0 - sig))).astype(jnp.bfloat16)
    grad_up = (grad32 * gate32 * sig).astype(jnp.bfloat16)
    piece_gate = lax.all_gather(grad_gate, "row", axis=0, tiled=True)
    piece_up = lax.all_gather(grad_up, "row", axis=0, tiled=True)
    acc_gate = contract_rows(inputs, piece_gate)
    acc_up = contract_rows(inputs, piece_up)
    part = contract_cols(piece_gate, gate_weight) + contract_cols(piece_up, up_weight)
    acc_gate, acc_up, partial_input = (acc_gate, acc_up, part)
    grad_input = reduce_input(partial_input)
    return (grad_input, acc_gate.astype(jnp.bfloat16), acc_up.astype(jnp.bfloat16))


def solution(mesh):
    return jax.shard_map(
        on_device,
        mesh=mesh,
        in_specs=(
            P(None, "row"),
            P("row", "col"),
            P("row", "col"),
            P("row", "col"),
            P("row", "col"),
            P("row", "col"),
        ),
        out_specs=(P("col", "row"), P("row", "col"), P("row", "col")),
        check_vma=False,
    )
```

profile of v0, /device:TPU:2, one launch (start us, length us, event | category | flops | bytes accessed | tf_op | source)
XLA Modules:
  0.0 560.5 jit_solution(11722829400085874786)
XLA Ops:
  7.2 0.0 copy-start
  7.2 0.0 all-gather.3.cloned.1.call-start
  7.2 1.9 fusion.10
  9.1 0.0 all-gather.3.cloned.1.call-update
  9.1 0.0 copy-start.1
  9.1 0.0 all-gather.5.cloned.1.call-start
  9.2 0.7 all-gather.5.cloned.1.call-update
  9.9 0.0 reduce-scatter.2.cloned.1.call-start
  9.9 74.9 %all-gather.3.cloned.1.call-done = bf16[1536,1152]{1,0:T(8,128)(2,1)} async-done(((bf16[48,1152]{1,0:T(8,128)(2,1)}), bf16[1536,1152]{1,0:T(8,128)(2,1)}) %all-gather.3.cloned.1.call-update) | async-done | bytes 3538960 | tf_op jit(solution)/shard_map/all_gather | solution.py:32
  84.9 3.3 fusion.11
  88.2 66.2 %all-gather.5.cloned.1.call-done = bf16[1536,1152]{1,0:T(8,128)(2,1)} async-done(((bf16[48,1152]{1,0:T(8,128)(2,1)}), bf16[1536,1152]{1,0:T(8,128)(2,1)}) %all-gather.5.cloned.1.call-update) | async-done | bytes 3538960 | tf_op jit(solution)/shard_map/all_gather | solution.py:33
  154.4 0.0 copy-done.1
  154.4 4.5 convolution_add_fusion
  158.9 0.0 reduce-scatter.2.cloned.1.call-update
  158.9 0.0 copy-done
  158.9 3.1 fusion.1
  162.0 1.1 copy.10
  163.1 3.1 fusion
  166.2 1.1 copy.9
  167.3 385.2 %reduce-scatter.2.cloned.1.call-done = f32[64,256]{1,0:T(8,128)} async-done(((f32[1536,256]{1,0:T(8,128)}), f32[64,256]{1,0:T(8,128)}) %reduce-scatter.2.cloned.1.call-update) | async-done | bytes 65552 | tf_op jit(solution)/shard_map/reduce_scatter | solution.py:20
  552.5 1.5 convert_element_type.35
Async XLA Ops:
  7.2 151.7 %copy-start = (bf16[1536,256]{1,0:T(8,128)(2,1)S(1)}, bf16[1536,256]{1,0:T(8,128)(2,1)}, u32[]{:S(2)}) copy-start(bf16[1536,256]{1,0:T(8,128)(2,1)} %param.6) | copy-start | bytes 2359300
  7.2 77.7 %all-gather.3.cloned.1.call-start = ((), (), s32[]{:S(2)}) async-start(), calls=%async_computation.1 | async-start | bytes 3649536 | tf_op jit(solution)/shard_map/all_gather | solution.py:32
  9.1 145.3 %copy-start.1 = (bf16[256,1152]{1,0:T(8,128)(2,1)S(1)}, bf16[256,1152]{1,0:T(8,128)(2,1)}, u32[]{:S(2)}) copy-start(bf16[256,1152]{1,0:T(8,128)(2,1)} %param.8) | copy-start | bytes 1769476
  9.1 145.3 %all-gather.5.cloned.1.call-start = ((), (), s32[]{:S(2)}) async-start(), calls=%async_computation.2 | async-start | bytes 3649536 | tf_op jit(solution)/shard_map/all_gather | solution.py:33
  9.9 542.7 %reduce-scatter.2.cloned.1.call-start = ((), (), s32[]{:S(2)}) async-start(), calls=%async_computation.3 | async-start | bytes 1638400 | tf_op jit(solution)/shard_map/reduce_scatter | solution.py:20
Sparse Core Ops, SparseCore 0:
  11.0 73.7 all-gather.2
  87.9 66.5 all-gather.4
  159.4 393.0 reduce-scatter.1
where the time goes:
time: 561 us
  waiting for transfers between devices  527 us (94%)
  matrix products  14.1 us (3%)
  between operations  13.8 us (2%)
    reduce_scatter x1, waiting for transfers between devices, reduce_input(): lax.psum_scatter(partial_input, 'col', scatter_dimension=0, tiled=True)  385 us
    all_gather x1, waiting for transfers between devices, on_device(): piece_gate = lax.all_gather(grad_gate, 'row', axis=0, tiled=True)  74.9 us
    all_gather x1, waiting for transfers between devices, on_device(): piece_up = lax.all_gather(grad_up, 'row', axis=0, tiled=True)  66.2 us
  transfers between devices with their start and end apart: 3, of which 3 were waited for; matrix products, arithmetic and copies ran while one was open for 2% of the time, Pallas kernels for 0%

commit v1 on v0

--- a/solution.py
+++ b/solution.py
@@ -17,9 +17,11 @@
 
 
 def reduce_input(partial_input):
-    return lax.psum_scatter(partial_input, "col", scatter_dimension=0, tiled=True).astype(
-        jnp.bfloat16
-    )
+    parts = lax.psum(1, "col")
+    rows, width = partial_input.shape
+    pieces = partial_input.reshape(parts, rows // parts, width)
+    pieces = lax.all_to_all(pieces, "col", 0, 0, tiled=False)
+    return pieces.sum(0).astype(jnp.bfloat16)
 
 
 def on_device(inputs, gate_weight, up_weight, gate_pre, up_pre, grad_act):
@@ -29,8 +31,9 @@
     sig = jax.nn.sigmoid(gate32)
     grad_gate = (grad32 * up32 * sig * (1.0 + gate32 * (1.0 - sig))).astype(jnp.bfloat16)
     grad_up = (grad32 * gate32 * sig).astype(jnp.bfloat16)
-    piece_gate = lax.all_gather(grad_gate, "row", axis=0, tiled=True)
-    piece_up = lax.all_gather(grad_up, "row", axis=0, tiled=True)
+    width = grad_gate.shape[1]
+    both = lax.all_gather(jnp.concatenate([grad_gate, grad_up], 1), "row", axis=0, tiled=True)
+    piece_gate, piece_up = both[:, :width], both[:, width:]
     acc_gate = contract_rows(inputs, piece_gate)
     acc_up = contract_rows(inputs, piece_up)
     part = contract_cols(piece_gate, gate_weight) + contract_cols(piece_up, up_weight)

time: 561 us -> 178 us (0.32)
  the two profiles are of different devices: /device:TPU:2 before, /device:TPU:8 now
where the time goes in v1:
time: 178 us; the launch traced here: 177 us
  waiting for transfers between devices  132 us (74%)
  starting transfers between devices  14.2 us (8%)
  between operations  14.1 us (8%)
  matrix products  12.3 us (7%)
  local copies, waits for them, and re-layouts  2.86 us (2%)
  other arithmetic  2.6 us (1%)
    all_gather x1, waiting for transfers between devices, on_device(): lax.all_gather(jnp.concatenate([grad_gate, grad_up], 1), 'row', axis=0, t...  81.1 us
    all_to_all x1, waiting for transfers between devices, reduce_input(): pieces = lax.all_to_all(pieces, 'col', 0, 0, tiled=False)  50.4 us
    all_to_all x1, starting transfers between devices, reduce_input(): pieces = lax.all_to_all(pieces, 'col', 0, 0, tiled=False)  14.1 us
    dot_general x2, matrix products, contract_rows(): lax.dot_general(left, right, (((0,), (0,)), ((), ())), preferred_element_...  6.26 us
    dot_general x2, matrix products, contract_cols(): lax.dot_general(left, right, (((1,), (1,)), ((), ())), preferred_element_...  5.99 us
  transfers between devices with their start and end apart: 2, of which 2 were waited for; matrix products, arithmetic and copies ran while one was open for 5% of the time, Pallas kernels for 0%

profile of v1, /device:TPU:8, one launch (start us, length us, event | category | flops | bytes accessed | tf_op | source)
XLA Modules:
  0.0 177.5 jit_solution(8925947465928226550)
XLA Ops:
  7.2 0.0 copy-start
  7.2 0.0 all-gather.2.cloned.1.call-start
  7.2 1.2 fusion.25
  8.4 0.7 pad_maximum_fusion
  9.1 0.0 all-gather.2.cloned.1.call-update
  9.1 0.0 copy-start.2
  9.2 81.1 %all-gather.2.cloned.1.call-done = bf16[1536,2304]{1,0:T(8,128)(2,1)} async-done(((bf16[48,2304]{1,0:T(8,128)(2,1)}), bf16[1536,2304]{1,0:T(8,128)(2,1)}) %all-gather.2.cloned.1.call-update) | async-done | bytes 7077904 | tf_op jit(solution)/shard_map/all_gather | solution.py:35
  90.3 0.0 copy-start.1
  90.3 3.5 %fusion.2 = f32[1536,256]{1,0:T(8,128)S(1)} fusion(bf16[256,1152]{1,0:T(8,128)(2,1)} %param.8, bf16[1536,2304]{1,0:T(8,128)(2,1)} %all-gather.2.cloned.1.call-done), kind=kOutput, calls=%fused_computation.2 | convolution fusion | flops 905969664 | bytes 5701632 | tf_op jit(solution)/shard_map/dot_general | solution.py:14
  93.8 0.0 copy-done.2
  93.8 0.7 copy-done.1
  94.5 2.5 %fusion.8 = f32[1536,256]{1,0:T(8,128)} fusion(f32[1536,256]{1,0:T(8,128)S(1)} %fusion.2, bf16[256,1152]{1,0:T(8,128)(2,1)S(1)} %copy-done.2, bf16[1536,2304]{1,0:T(8,128)(2,1)S(1)} %copy-done.1), kind=kOutput, calls=%fused_computation.8 | convolution fusion | flops 906362880 | bytes 7274496 | tf_op jit(solution)/shard_map/dot_general | solution.py:14
  97.0 14.1 %all-to-all-start = ((f32[24,64,256]{2,1,0:T(8,128)}), f32[24,64,256]{2,1,0:T(8,128)S(1)}, u32[]{:S(2)}, u32[]{:S(2)}) async-start(f32[24,64,256]{2,1,0:T(8,128)} %bitcast.9), calls=%async_computation | async-start | bytes 3145728 | tf_op jit(solution)/shard_map/all_to_all | solution.py:23
  111.1 0.0 copy-done
  111.2 3.1 %fusion.20 = bf16[256,1152]{0,1:T(8,128)(2,1)S(1)} fusion(bf16[1536,256]{1,0:T(8,128)(2,1)S(1)} %copy-done, bf16[1536,2304]{1,0:T(8,128)(2,1)} %all-gather.2.cloned.1.call-done), kind=kOutput, calls=%fused_computation.12 | convolution fusion | flops 906264576 | bytes 4915200 | tf_op jit(solution)/shard_map/dot_general | solution.py:8
  114.3 1.1 copy.9
  115.3 3.1 %fusion.17 = bf16[256,1152]{0,1:T(8,128)(2,1)S(1)} fusion(bf16[1536,256]{1,0:T(8,128)(2,1)S(1)} %copy-done, bf16[1536,2304]{1,0:T(8,128)(2,1)} %all-gather.2.cloned.1.call-done), kind=kOutput, calls=%fused_computation.11 | convolution fusion | flops 906264576 | bytes 4915200 | tf_op jit(solution)/shard_map/dot_general | solution.py:8
  118.5 1.1 copy.10
  119.5 50.4 %all-to-all-done = f32[24,64,256]{2,1,0:T(8,128)S(1)} async-done(((f32[24,64,256]{2,1,0:T(8,128)}), f32[24,64,256]{2,1,0:T(8,128)S(1)}, u32[]{:S(2)}, u32[]{:S(2)}) %all-to-all-start) | async-done | bytes 1572896 | tf_op jit(solution)/shard_map/all_to_all | solution.py:23
  169.9 0.7 reduce_sum.9
Async XLA Ops:
  7.2 104.0 %copy-start = (bf16[1536,256]{1,0:T(8,128)(2,1)S(1)}, bf16[1536,256]{1,0:T(8,128)(2,1)}, u32[]{:S(2)}) copy-start(bf16[1536,256]{1,0:T(8,128)(2,1)} %param.6) | copy-start | bytes 2359300
  7.2 83.1 %all-gather.2.cloned.1.call-start = ((), (), s32[]{:S(2)}) async-start(), calls=%async_computation.1 | async-start | bytes 7299072 | tf_op jit(solution)/shard_map/all_gather | solution.py:35
  9.1 84.6 %copy-start.2 = (bf16[256,1152]{1,0:T(8,128)(2,1)S(1)}, bf16[256,1152]{1,0:T(8,128)(2,1)}, u32[]{:S(2)}) copy-start(bf16[256,1152]{1,0:T(8,128)(2,1)} %param.7) | copy-start | bytes 1769476
  90.3 4.2 %copy-start.1 = (bf16[1536,2304]{1,0:T(8,128)(2,1)S(1)}, bf16[1536,2304]{1,0:T(8,128)(2,1)}, u32[]{:S(2)}) copy-start(bf16[1536,2304]{1,0:T(8,128)(2,1)} %all-gather.2.cloned.1.call-done) | copy-start | bytes 21233668
  97.0 72.9 %all-to-all-start = ((f32[24,64,256]{2,1,0:T(8,128)}), f32[24,64,256]{2,1,0:T(8,128)S(1)}, u32[]{:S(2)}, u32[]{:S(2)}) async-start(f32[24,64,256]{2,1,0:T(8,128)} %bitcast.9), calls=%async_computation | async-start | bytes 3145728 | tf_op jit(solution)/shard_map/all_to_all | solution.py:23
Sparse Core Ops, SparseCore 0:
  11.0 79.2 all-gather.1

commit v2 on v1

--- a/solution.py
+++ b/solution.py
@@ -2,6 +2,9 @@
 import jax.numpy as jnp
 from jax import lax
 from jax.sharding import PartitionSpec as P
+
+PERIOD = 16
+CHUNKS = 2
 
 
 def contract_rows(left, right):
@@ -16,12 +19,18 @@
     )
 
 
+def take_chunk(rows, index):
+    size = PERIOD // CHUNKS
+    grouped = rows.reshape(rows.shape[0] // PERIOD, PERIOD, rows.shape[1])
+    return grouped[:, index * size:(index + 1) * size].reshape(-1, rows.shape[1])
+
+
 def reduce_input(partial_input):
     parts = lax.psum(1, "col")
     rows, width = partial_input.shape
     pieces = partial_input.reshape(parts, rows // parts, width)
     pieces = lax.all_to_all(pieces, "col", 0, 0, tiled=False)
-    return pieces.sum(0).astype(jnp.bfloat16)
+    return pieces.sum(0)
 
 
 def on_device(inputs, gate_weight, up_weight, gate_pre, up_pre, grad_act):
@@ -32,13 +41,22 @@
     grad_gate = (grad32 * up32 * sig * (1.0 + gate32 * (1.0 - sig))).astype(jnp.bfloat16)
     grad_up = (grad32 * gate32 * sig).astype(jnp.bfloat16)
     width = grad_gate.shape[1]
-    both = lax.all_gather(jnp.concatenate([grad_gate, grad_up], 1), "row", axis=0, tiled=True)
-    piece_gate, piece_up = both[:, :width], both[:, width:]
-    acc_gate = contract_rows(inputs, piece_gate)
-    acc_up = contract_rows(inputs, piece_up)
-    part = contract_cols(piece_gate, gate_weight) + contract_cols(piece_up, up_weight)
-    acc_gate, acc_up, partial_input = (acc_gate, acc_up, part)
-    grad_input = reduce_input(partial_input)
+    both = jnp.concatenate([grad_gate, grad_up], 1)
+    acc_gate = None
+    acc_up = None
+    outs = []
+    for index in range(CHUNKS):
+        piece = lax.all_gather(take_chunk(both, index), "row", axis=0, tiled=True)
+        piece_gate, piece_up = piece[:, :width], piece[:, width:]
+        rows = take_chunk(inputs, index)
+        step_gate = contract_rows(rows, piece_gate)
+        step_up = contract_rows(rows, piece_up)
+        acc_gate = step_gate if acc_gate is None else acc_gate + step_gate
+        acc_up = step_up if acc_up is None else acc_up + step_up
+        part = contract_cols(piece_gate, gate_weight) + contract_cols(piece_up, up_weight)
+        out = reduce_input(part)
+        outs.append(out.reshape(-1, PERIOD // CHUNKS, out.shape[1]))
+    grad_input = jnp.stack(outs, 1).reshape(-1, outs[0].shape[2]).astype(jnp.bfloat16)
     return (grad_input, acc_gate.astype(jnp.bfloat16), acc_up.astype(jnp.bfloat16))
 
 

time: 178 us -> 227 us (1.28)
  waiting for transfers between devices: 132 us -> 160 us
  starting transfers between devices: 14.2 us -> 32.8 us
    all_gather x1 -> x2, waiting for transfers between devices: 81.1 us -> 132 us  [on_device(): piece = lax.all_gather(take_chunk(both, index), 'row', axis=0, tiled=True)]
    all_to_all x1 -> x2, waiting for transfers between devices: 50.4 us -> 27.3 us  [reduce_input(): pieces = lax.all_to_all(pieces, 'col', 0, 0, tiled=False)]
    all_to_all x1 -> x2, starting transfers between devices: 14.1 us -> 32.8 us  [reduce_input(): pieces = lax.all_to_all(pieces, 'col', 0, 0, tiled=False)]
    dot_general x2 -> x4, matrix products: 5.99 us -> 7.96 us  [contract_cols(): lax.dot_general(left, right, (((1,), (1,)), ((), ())), preferred_element_...]
    dot_general x2 -> x4, matrix products: 6.26 us -> 5.97 us  [contract_rows(): lax.dot_general(left, right, (((0,), (0,)), ((), ())), preferred_element_...]
  transfers between devices with their start and end apart: 2 -> 4, of which waited for: 2 -> 3; matrix products, arithmetic and copies ran while one was open for 5% -> 7% of each run, Pallas kernels for 0% -> 0%
where the time goes in v2:
time: 227 us; the launch traced here: 226 us
  waiting for transfers between devices  160 us (70%)
  starting transfers between devices  32.8 us (14%)
  between operations  14.2 us (6%)
  matrix products  13.9 us (6%)
  local copies, waits for them, and re-layouts  3.64 us (2%)
    all_gather x2, waiting for transfers between devices, on_device(): piece = lax.all_gather(take_chunk(both, index), 'row', axis=0, tiled=True)  132 us
    all_to_all x2, starting transfers between devices, reduce_input(): pieces = lax.all_to_all(pieces, 'col', 0, 0, tiled=False)  32.8 us
    all_to_all x2, waiting for transfers between devices, reduce_input(): pieces = lax.all_to_all(pieces, 'col', 0, 0, tiled=False)  27.3 us
    dot_general x4, matrix products, contract_cols(): lax.dot_general(left, right, (((1,), (1,)), ((), ())), preferred_element_...  7.96 us
    dot_general x4, matrix products, contract_rows(): lax.dot_general(left, right, (((0,), (0,)), ((), ())), preferred_element_...  5.97 us
  transfers between devices with their start and end apart: 4, of which 3 were waited for; matrix products, arithmetic and copies ran while one was open for 7% of the time, Pallas kernels for 0%

profile of v2, /device:TPU:8, one launch (start us, length us, event | category | flops | bytes accessed | tf_op | source)
XLA Modules:
  0.0 226.3 jit_solution(10540112143215304459)
XLA Ops:
  7.2 1.2 fusion.26
  8.4 0.7 slice_bitcast_fusion.7
  9.2 0.7 all-gather.5.cloned.1.call-update
  9.9 74.9 %all-gather.3.cloned.1.call-done = bf16[768,2304]{1,0:T(8,128)(2,1)} async-done(((bf16[24,2304]{1,0:T(8,128)(2,1)}), bf16[768,2304]{1,0:T(8,128)(2,1)}) %all-gather.3.cloned.1.call-update) | async-done | bytes 3538960 | tf_op jit(solution)/shard_map/all_gather | solution.py:49
  84.8 2.3 %fusion.12 = f32[768,256]{1,0:T(8,128)S(1)} fusion(bf16[256,1152]{1,0:T(8,128)(2,1)S(1)} %copy-done, bf16[768,2304]{1,0:T(8,128)(2,1)} %all-gather.3.cloned.1.call-done), kind=kOutput, calls=%fused_computation.14 | convolution fusion | flops 452984832 | bytes 3145728 | tf_op jit(solution)/shard_map/dot_general | solution.py:17
  87.1 0.2 copy-done.1
  87.3 1.7 fusion.18
  89.0 13.8 %all-to-all-start = ((f32[24,32,256]{2,1,0:T(8,128)}), f32[24,32,256]{2,1,0:T(8,128)S(1)}, u32[]{:S(2)}, u32[]{:S(2)}) async-start(f32[24,32,256]{2,1,0:T(8,128)} %bitcast.2), calls=%async_computation | async-start | bytes 1572864 | tf_op jit(solution)/shard_map/all_to_all | solution.py:32
  102.8 56.9 %all-gather.5.cloned.1.call-done = bf16[768,2304]{1,0:T(8,128)(2,1)} async-done(((bf16[24,2304]{1,0:T(8,128)(2,1)}), bf16[768,2304]{1,0:T(8,128)(2,1)}) %all-gather.5.cloned.1.call-update) | async-done | bytes 3538960 | tf_op jit(solution)/shard_map/all_gather | solution.py:49
  159.8 2.3 %fusion.5 = f32[768,256]{1,0:T(8,128)S(1)} fusion(bf16[256,1152]{1,0:T(8,128)(2,1)S(1)} %copy-done, bf16[768,2304]{1,0:T(8,128)(2,1)} %all-gather.5.cloned.1.call-done), kind=kOutput, calls=%fused_computation.7 | convolution fusion | flops 452984832 | bytes 3145728 | tf_op jit(solution)/shard_map/dot_general | solution.py:17
  162.1 0.2 copy-done.2
  162.3 1.6 fusion.21
  163.9 18.9 %all-to-all-start.1 = ((f32[24,32,256]{2,1,0:T(8,128)}), f32[24,32,256]{2,1,0:T(8,128)S(1)}, u32[]{:S(2)}, u32[]{:S(2)}) async-start(f32[24,32,256]{2,1,0:T(8,128)} %bitcast.5), calls=%async_computation.1 | async-start | bytes 1572864 | tf_op jit(solution)/shard_map/all_to_all | solution.py:32
  182.9 2.3 %fusion.10 = f32[1152,256]{1,0:T(8,128)S(1)} fusion(bf16[768,2304]{1,0:T(8,128)(2,1)} %all-gather.3.cloned.1.call-done, bf16[96,16,256]{2,1,0:T(8,128)(2,1)S(1)} %bitcast.35), kind=kOutput, calls=%fused_computation.12 | convolution fusion | flops 452984832 | bytes 3342336 | tf_op jit(solution)/shard_map/dot_general | solution.py:11
  185.2 0.2 copy-done.3
  185.4 0.7 fusion.2
  186.1 1.1 copy.10
  187.1 2.3 %fusion.14 = f32[1152,256]{1,0:T(8,128)S(1)} fusion(bf16[768,2304]{1,0:T(8,128)(2,1)} %all-gather.3.cloned.1.call-done, bf16[96,16,256]{2,1,0:T(8,128)(2,1)S(1)} %bitcast.37), kind=kOutput, calls=%fused_computation.16 | convolution fusion | flops 452984832 | bytes 3342336 | tf_op jit(solution)/shard_map/dot_general | solution.py:11
  189.4 0.2 copy-done.4
  189.7 0.7 fusion.3
  190.4 1.1 copy.9
  191.4 0.1 reduce_sum.18
  191.5 27.3 %all-to-all-done.1 = f32[24,32,256]{2,1,0:T(8,128)S(1)} async-done(((f32[24,32,256]{2,1,0:T(8,128)}), f32[24,32,256]{2,1,0:T(8,128)S(1)}, u32[]{:S(2)}, u32[]{:S(2)}) %all-to-all-start.1) | async-done | bytes 786464 | tf_op jit(solution)/shard_map/all_to_all | solution.py:32
  218.8 0.6 pad_maximum_fusion.1
  (16 shorter events, 0.2 us)
Async XLA Ops:
  7.2 77.6 %copy-start = (bf16[256,1152]{1,0:T(8,128)(2,1)S(1)}, bf16[256,1152]{1,0:T(8,128)(2,1)}, u32[]{:S(2)}) copy-start(bf16[256,1152]{1,0:T(8,128)(2,1)} %param.8) | copy-start | bytes 1769476
  7.2 77.6 %all-gather.3.cloned.1.call-start = ((), (), s32[]{:S(2)}) async-start(), calls=%async_computation.2 | async-start | bytes 3649536 | tf_op jit(solution)/shard_map/all_gather | solution.py:49
  8.4 78.7 %copy-start.6 = (bf16[256,1152]{1,0:T(8,128)(2,1)S(1)}, bf16[256,1152]{1,0:T(8,128)(2,1)}, u32[]{:S(2)}) copy-start(bf16[256,1152]{1,0:T(8,128)(2,1)} %param.7) | copy-start | bytes 1769476
  9.2 150.6 %all-gather.5.cloned.1.call-start = ((), (), s32[]{:S(2)}) async-start(), calls=%async_computation.3 | async-start | bytes 3649536 | tf_op jit(solution)/shard_map/all_gather | solution.py:49
  84.8 2.5 %copy-start.1 = (bf16[768,2304]{1,0:T(8,128)(2,1)S(1)}, bf16[768,2304]{1,0:T(8,128)(2,1)}, u32[]{:S(2)}) copy-start(bf16[768,2304]{1,0:T(8,128)(2,1)} %all-gather.3.cloned.1.call-done) | copy-start | bytes 10616836
  89.0 74.9 %all-to-all-start = ((f32[24,32,256]{2,1,0:T(8,128)}), f32[24,32,256]{2,1,0:T(8,128)S(1)}, u32[]{:S(2)}, u32[]{:S(2)}) async-start(f32[24,32,256]{2,1,0:T(8,128)} %bitcast.2), calls=%async_computation | async-start | bytes 1572864 | tf_op jit(solution)/shard_map/all_to_all | solution.py:32
  159.8 2.5 %copy-start.2 = (bf16[768,2304]{1,0:T(8,128)(2,1)S(1)}, bf16[768,2304]{1,0:T(8,128)(2,1)}, u32[]{:S(2)}) copy-start(bf16[768,2304]{1,0:T(8,128)(2,1)} %all-gather.5.cloned.1.call-done) | copy-start | bytes 10616836
  162.3 20.5 %copy-start.5 = (bf16[1536,256]{1,0:T(8,128)(2,1)S(1)}, bf16[1536,256]{1,0:T(8,128)(2,1)}, u32[]{:S(2)}) copy-start(bf16[1536,256]{1,0:T(8,128)(2,1)} %param.6) | copy-start | bytes 2359300
  163.9 54.9 %all-to-all-start.1 = ((f32[24,32,256]{2,1,0:T(8,128)}), f32[24,32,256]{2,1,0:T(8,128)S(1)}, u32[]{:S(2)}, u32[]{:S(2)}) async-start(f32[24,32,256]{2,1,0:T(8,128)} %bitcast.5), calls=%async_computation.1 | async-start | bytes 1572864 | tf_op jit(solution)/shard_map/all_to_all | solution.py:32
  182.9 2.5 %copy-start.3 = (bf16[768,2304]{1,0:T(8,128)(2,1)S(1)}, bf16[768,2304]{1,0:T(8,128)(2,1)}, u32[]{:S(2)}) copy-start(bf16[768,2304]{1,0:T(8,128)(2,1)} %all-gather.5.cloned.1.call-done) | copy-start | bytes 10616836
  187.1 2.5 %copy-start.4 = (bf16[768,2304]{1,0:T(8,128)(2,1)S(1)}, bf16[768,2304]{1,0:T(8,128)(2,1)}, u32[]{:S(2)}) copy-start(bf16[768,2304]{1,0:T(8,128)(2,1)} %all-gather.5.cloned.1.call-done) | copy-start | bytes 10616836
Sparse Core Ops, SparseCore 0:
  11.0 73.7 all-gather.2
  87.8 71.9 all-gather.4

commit v3 on v1

--- a/solution.py
+++ b/solution.py
@@ -33,11 +33,10 @@
     grad_up = (grad32 * gate32 * sig).astype(jnp.bfloat16)
     width = grad_gate.shape[1]
     both = lax.all_gather(jnp.concatenate([grad_gate, grad_up], 1), "row", axis=0, tiled=True)
-    piece_gate, piece_up = both[:, :width], both[:, width:]
-    acc_gate = contract_rows(inputs, piece_gate)
-    acc_up = contract_rows(inputs, piece_up)
-    part = contract_cols(piece_gate, gate_weight) + contract_cols(piece_up, up_weight)
-    acc_gate, acc_up, partial_input = (acc_gate, acc_up, part)
+    acc = contract_rows(inputs, both)
+    acc_gate, acc_up = acc[:, :width], acc[:, width:]
+    weights = jnp.concatenate([gate_weight, up_weight], 1)
+    partial_input = contract_cols(both, weights)
     grad_input = reduce_input(partial_input)
     return (grad_input, acc_gate.astype(jnp.bfloat16), acc_up.astype(jnp.bfloat16))
 

time: 178 us -> 177 us (level)
    dot_general x2 -> x1, matrix products: 6.26 us -> 5.05 us  [contract_rows(): lax.dot_general(left, right, (((0,), (0,)), ((), ())), preferred_element_...]
    dot_general x2 -> x1, matrix products: 5.99 us -> 6.5 us  [contract_cols(): lax.dot_general(left, right, (((1,), (1,)), ((), ())), preferred_element_...]
  transfers between devices with their start and end apart: 2 -> 2, of which waited for: 2 -> 2; matrix products, arithmetic and copies ran while one was open for 5% -> 4% of each run, Pallas kernels for 0% -> 0%
where the time goes in v3:
time: 177 us
  waiting for transfers between devices  133 us (75%)
  starting transfers between devices  14.2 us (8%)
  between operations  14.1 us (8%)
  matrix products  11.6 us (7%)
  other arithmetic  2.6 us (1%)
  local copies, waits for them, and re-layouts  2.2 us (1%)
    all_gather x1, waiting for transfers between devices, on_device(): lax.all_gather(jnp.concatenate([grad_gate, grad_up], 1), 'row', axis=0, t...  81.1 us
    all_to_all x1, waiting for transfers between devices, reduce_input(): pieces = lax.all_to_all(pieces, 'col', 0, 0, tiled=False)  51.5 us
    all_to_all x1, starting transfers between devices, reduce_input(): pieces = lax.all_to_all(pieces, 'col', 0, 0, tiled=False)  14.1 us
    dot_general x1, matrix products, contract_cols(): lax.dot_general(left, right, (((1,), (1,)), ((), ())), preferred_element_...  6.5 us
    dot_general x1, matrix products, contract_rows(): lax.dot_general(left, right, (((0,), (0,)), ((), ())), preferred_element_...  5.05 us
  transfers between devices with their start and end apart: 2, of which 2 were waited for; matrix products, arithmetic and copies ran while one was open for 4% of the time, Pallas kernels for 0%

profile of v3, /device:TPU:8, one launch (start us, length us, event | category | flops | bytes accessed | tf_op | source)
XLA Modules:
  0.0 177.2 jit_solution(9913171895330527363)
XLA Ops:
  7.2 0.0 copy-start
  7.2 0.0 all-gather.2.cloned.1.call-start
  7.2 1.2 fusion.7
  8.4 0.7 pad_maximum_fusion
  9.1 0.0 all-gather.2.cloned.1.call-update
  9.1 81.1 %all-gather.2.cloned.1.call-done = bf16[1536,2304]{1,0:T(8,128)(2,1)} async-done(((bf16[48,2304]{1,0:T(8,128)(2,1)}), bf16[1536,2304]{1,0:T(8,128)(2,1)}) %all-gather.2.cloned.1.call-update) | async-done | bytes 7077904 | tf_op jit(solution)/shard_map/all_gather | solution.py:35
  90.3 6.5 %fusion.1 = f32[1536,256]{1,0:T(8,128)} fusion(bf16[1536,2304]{1,0:T(8,128)(2,1)} %all-gather.2.cloned.1.call-done, bf16[256,1152]{1,0:T(8,128)(2,1)} %param.8, bf16[256,1152]{1,0:T(8,128)(2,1)} %param.7), kind=kOutput, calls=%fused_computation.2 | convolution fusion | flops 1814298624 | bytes 9830400 | tf_op jit(solution)/shard_map/dot_general | solution.py:14
  96.8 14.1 %all-to-all-start = ((f32[24,64,256]{2,1,0:T(8,128)}), f32[24,64,256]{2,1,0:T(8,128)S(1)}, u32[]{:S(2)}, u32[]{:S(2)}) async-start(f32[24,64,256]{2,1,0:T(8,128)} %bitcast.6), calls=%async_computation | async-start | bytes 3145728 | tf_op jit(solution)/shard_map/all_to_all | solution.py:23
  110.9 0.0 copy-done
  110.9 5.1 %fusion = bf16[256,2304]{0,1:T(8,128)(2,1)S(1)} fusion(bf16[1536,2304]{1,0:T(8,128)(2,1)} %all-gather.2.cloned.1.call-done, bf16[1536,256]{1,0:T(8,128)(2,1)S(1)} %copy-done), kind=kOutput, calls=%fused_computation.1 | convolution fusion | flops 1812529152 | bytes 9043968 | tf_op jit(solution)/shard_map/dot_general | solution.py:8
  116.0 0.1 fusion.15
  116.1 1.1 copy.10
  117.1 1.1 copy.9
  118.2 51.5 %all-to-all-done = f32[24,64,256]{2,1,0:T(8,128)S(1)} async-done(((f32[24,64,256]{2,1,0:T(8,128)}), f32[24,64,256]{2,1,0:T(8,128)S(1)}, u32[]{:S(2)}, u32[]{:S(2)}) %all-to-all-start) | async-done | bytes 1572896 | tf_op jit(solution)/shard_map/all_to_all | solution.py:23
  169.7 0.7 reduce_sum.9
Async XLA Ops:
  7.2 103.7 %copy-start = (bf16[1536,256]{1,0:T(8,128)(2,1)S(1)}, bf16[1536,256]{1,0:T(8,128)(2,1)}, u32[]{:S(2)}) copy-start(bf16[1536,256]{1,0:T(8,128)(2,1)} %param.6) | copy-start | bytes 2359300
  7.2 83.1 %all-gather.2.cloned.1.call-start = ((), (), s32[]{:S(2)}) async-start(), calls=%async_computation.1 | async-start | bytes 7299072 | tf_op jit(solution)/shard_map/all_gather | solution.py:35
  96.8 72.9 %all-to-all-start = ((f32[24,64,256]{2,1,0:T(8,128)}), f32[24,64,256]{2,1,0:T(8,128)S(1)}, u32[]{:S(2)}, u32[]{:S(2)}) async-start(f32[24,64,256]{2,1,0:T(8,128)} %bitcast.6), calls=%async_computation | async-start | bytes 3145728 | tf_op jit(solution)/shard_map/all_to_all | solution.py:23
Sparse Core Ops, SparseCore 0:
  11.0 79.2 all-gather.1

commit v4 on v3

--- a/solution.py
+++ b/solution.py
@@ -1,7 +1,10 @@
 import jax
 import jax.numpy as jnp
 from jax import lax
+from jax.experimental import pallas as pl
 from jax.sharding import PartitionSpec as P
+
+TILE_ROWS = 768
 
 
 def contract_rows(left, right):
@@ -14,6 +17,38 @@
     return lax.dot_general(
         left, right, (((1,), (1,)), ((), ())), preferred_element_type=jnp.float32
     )
+
+
+def input_kernel(both_ref, gate_ref, up_ref, out_ref):
+    width = gate_ref.shape[1]
+    dims = (((1,), (1,)), ((), ()))
+    out_ref[...] = lax.dot_general(
+        both_ref[:, :width], gate_ref[...], dims, preferred_element_type=jnp.float32
+    ) + lax.dot_general(
+        both_ref[:, width:], up_ref[...], dims, preferred_element_type=jnp.float32
+    )
+
+
+def partial_input_of(both, gate_weight, up_weight):
+    rows, width = both.shape
+    features = gate_weight.shape[0]
+    tile = TILE_ROWS if rows % TILE_ROWS == 0 else rows
+    return pl.pallas_call(
+        input_kernel,
+        grid=(rows // tile,),
+        in_specs=[
+            pl.BlockSpec((tile, width), lambda i: (i, 0)),
+            pl.BlockSpec(gate_weight.shape, lambda i: (0, 0)),
+            pl.BlockSpec(up_weight.shape, lambda i: (0, 0)),
+        ],
+        out_specs=pl.BlockSpec((tile, features), lambda i: (i, 0)),
+        out_shape=jax.ShapeDtypeStruct((rows, features), jnp.float32),
+        cost_estimate=pl.CostEstimate(
+            flops=2 * rows * width * features,
+            bytes_accessed=2 * (rows * width + 2 * features * gate_weight.shape[1]) + 4 * rows * features,
+            transcendentals=0,
+        ),
+    )(both, gate_weight, up_weight)
 
 
 def reduce_input(partial_input):
@@ -35,8 +70,7 @@
     both = lax.all_gather(jnp.concatenate([grad_gate, grad_up], 1), "row", axis=0, tiled=True)
     acc = contract_rows(inputs, both)
     acc_gate, acc_up = acc[:, :width], acc[:, width:]
-    weights = jnp.concatenate([gate_weight, up_weight], 1)
-    partial_input = contract_cols(both, weights)
+    partial_input = partial_input_of(both, gate_weight, up_weight)
     grad_input = reduce_input(partial_input)
     return (grad_input, acc_gate.astype(jnp.bfloat16), acc_up.astype(jnp.bfloat16))
 

time: 177 us -> 177 us (level)
  matrix products: 11.6 us -> 5.05 us
  Pallas kernels: 0 us -> 5.68 us
    dot_general x1 -> x0, matrix products: 6.5 us -> none  [contract_cols(): lax.dot_general(left, right, (((1,), (1,)), ((), ())), preferred_element_...]
    pallas_call x0 -> x1, Pallas kernels: none -> 5.68 us  [partial_input_of(): pl.pallas_call(input_kernel, grid=(rows // tile,), in_specs=[pl.BlockSpec...]
where the time goes in v4:
time: 177 us; the launch traced here: 176 us
  waiting for transfers between devices  133 us (75%)
  starting transfers between devices  14.2 us (8%)
  between operations  14.1 us (8%)
  Pallas kernels  5.68 us (3%)
  matrix products  5.05 us (3%)
  other arithmetic  2.6 us (1%)
  local copies, waits for them, and re-layouts  2.2 us (1%)
    all_gather x1, waiting for transfers between devices, on_device(): lax.all_gather(jnp.concatenate([grad_gate, grad_up], 1), 'row', axis=0, t...  81.1 us
    all_to_all x1, waiting for transfers between devices, reduce_input(): pieces = lax.all_to_all(pieces, 'col', 0, 0, tiled=False)  51.5 us
    all_to_all x1, starting transfers between devices, reduce_input(): pieces = lax.all_to_all(pieces, 'col', 0, 0, tiled=False)  14.1 us
    pallas_call x1, Pallas kernels, partial_input_of(): pl.pallas_call(input_kernel, grid=(rows // tile,), in_specs=[pl.BlockSpec...  5.68 us
    dot_general x1, matrix products, contract_rows(): lax.dot_general(left, right, (((0,), (0,)), ((), ())), preferred_element_...  5.05 us
  transfers between devices with their start and end apart: 2, of which 2 were waited for; matrix products, arithmetic and copies ran while one was open for 4% of the time, Pallas kernels for 0%

profile of v4, /device:TPU:8, one launch (start us, length us, event | category | flops | bytes accessed | tf_op | source)
XLA Modules:
  0.0 176.4 jit_solution(5325608620347313198)
XLA Ops:
  7.2 0.0 copy-start
  7.2 0.0 all-gather.2.cloned.1.call-start
  7.2 1.2 fusion.3
  8.4 0.7 pad_maximum_fusion
  9.1 0.0 all-gather.2.cloned.1.call-update
  9.1 81.1 %all-gather.2.cloned.1.call-done.both_ref = bf16[1536,2304]{1,0:T(8,128)(2,1)} async-done(((bf16[48,2304]{1,0:T(8,128)(2,1)}), bf16[1536,2304]{1,0:T(8,128)(2,1)}) %all-gather.2.cloned.1.call-update) | async-done | bytes 7077904 | tf_op jit(solution)/shard_map/all_gather | solution.py:70
  90.3 5.7 %shard_map.85 = f32[1536,256]{1,0:T(8,128)} custom-call(bf16[1536,2304]{1,0:T(8,128)(2,1)} %all-gather.2.cloned.1.call-done.both_ref, bf16[256,1152]{1,0:T(8,128)(2,1)} %gate_ref.1, bf16[256,1152]{1,0:T(8,128)(2,1)} %up_ref.1), custom_call_target="tpu_custom_call" | custom-call | flops 1811939328 | bytes 9830400 | tf_op jit(solution)/shard_map/pallas_call | solution.py:36
  96.0 14.1 %all-to-all-start = ((f32[24,64,256]{2,1,0:T(8,128)}), f32[24,64,256]{2,1,0:T(8,128)S(1)}, u32[]{:S(2)}, u32[]{:S(2)}) async-start(f32[24,64,256]{2,1,0:T(8,128)} %bitcast.5), calls=%async_computation | async-start | bytes 3145728 | tf_op jit(solution)/shard_map/all_to_all | solution.py:58
  110.1 0.0 copy-done
  110.1 5.1 %fusion = bf16[256,2304]{0,1:T(8,128)(2,1)S(1)} fusion(bf16[1536,2304]{1,0:T(8,128)(2,1)} %all-gather.2.cloned.1.call-done.both_ref, bf16[1536,256]{1,0:T(8,128)(2,1)S(1)} %copy-done), kind=kOutput, calls=%fused_computation.1 | convolution fusion | flops 1812529152 | bytes 9043968 | tf_op jit(solution)/shard_map/dot_general | solution.py:11
  115.1 0.1 fusion.10
  115.2 1.1 copy.10
  116.3 1.1 copy.9
  117.3 51.5 %all-to-all-done = f32[24,64,256]{2,1,0:T(8,128)S(1)} async-done(((f32[24,64,256]{2,1,0:T(8,128)}), f32[24,64,256]{2,1,0:T(8,128)S(1)}, u32[]{:S(2)}, u32[]{:S(2)}) %all-to-all-start) | async-done | bytes 1572896 | tf_op jit(solution)/shard_map/all_to_all | solution.py:58
  168.9 0.7 reduce_sum.9
Async XLA Ops:
  7.2 102.9 %copy-start = (bf16[1536,256]{1,0:T(8,128)(2,1)S(1)}, bf16[1536,256]{1,0:T(8,128)(2,1)}, u32[]{:S(2)}) copy-start(bf16[1536,256]{1,0:T(8,128)(2,1)} %param.6) | copy-start | bytes 2359300
  7.2 83.1 %all-gather.2.cloned.1.call-start = ((), (), s32[]{:S(2)}) async-start(), calls=%async_computation.1 | async-start | bytes 7299072 | tf_op jit(solution)/shard_map/all_gather | solution.py:70
  96.0 72.9 %all-to-all-start = ((f32[24,64,256]{2,1,0:T(8,128)}), f32[24,64,256]{2,1,0:T(8,128)S(1)}, u32[]{:S(2)}, u32[]{:S(2)}) async-start(f32[24,64,256]{2,1,0:T(8,128)} %bitcast.5), calls=%async_computation | async-start | bytes 3145728 | tf_op jit(solution)/shard_map/all_to_all | solution.py:58
Sparse Core Ops, SparseCore 0:
  11.0 79.2 all-gather.1

commit v5 on v4

--- a/solution.py
+++ b/solution.py
@@ -60,14 +60,16 @@
 
 
 def on_device(inputs, gate_weight, up_weight, gate_pre, up_pre, grad_act):
-    gate32 = gate_pre.astype(jnp.float32)
-    up32 = up_pre.astype(jnp.float32)
-    grad32 = grad_act.astype(jnp.float32)
+    width = gate_pre.shape[1]
+    gate32 = jnp.concatenate([gate_pre, gate_pre], 1).astype(jnp.float32)
+    up32 = jnp.concatenate([up_pre, up_pre], 1).astype(jnp.float32)
+    grad32 = jnp.concatenate([grad_act, grad_act], 1).astype(jnp.float32)
     sig = jax.nn.sigmoid(gate32)
-    grad_gate = (grad32 * up32 * sig * (1.0 + gate32 * (1.0 - sig))).astype(jnp.bfloat16)
-    grad_up = (grad32 * gate32 * sig).astype(jnp.bfloat16)
-    width = grad_gate.shape[1]
-    both = lax.all_gather(jnp.concatenate([grad_gate, grad_up], 1), "row", axis=0, tiled=True)
+    is_gate = lax.broadcasted_iota(jnp.int32, gate32.shape, 1) < width
+    grad_both = jnp.where(
+        is_gate, grad32 * up32 * sig * (1.0 + gate32 * (1.0 - sig)), grad32 * gate32 * sig
+    ).astype(jnp.bfloat16)
+    both = lax.all_gather(grad_both, "row", axis=0, tiled=True)
     acc = contract_rows(inputs, both)
     acc_gate, acc_up = acc[:, :width], acc[:, width:]
     partial_input = partial_input_of(both, gate_weight, up_weight)

time: 177 us -> 177 us (level)
  no operation moved by 1% of the time
where the time goes in v5:
time: 177 us; the launch traced here: 176 us
  waiting for transfers between devices  132 us (75%)
  starting transfers between devices  14.2 us (8%)
  between operations  14.1 us (8%)
  Pallas kernels  5.67 us (3%)
  matrix products  5.05 us (3%)
  other arithmetic  2.87 us (2%)
  local copies, waits for them, and re-layouts  2.2 us (1%)
    all_gather x1, waiting for transfers between devices, on_device(): both = lax.all_gather(grad_both, 'row', axis=0, tiled=True)  80.9 us
    all_to_all x1, waiting for transfers between devices, reduce_input(): pieces = lax.all_to_all(pieces, 'col', 0, 0, tiled=False)  51.5 us
    all_to_all x1, starting transfers between devices, reduce_input(): pieces = lax.all_to_all(pieces, 'col', 0, 0, tiled=False)  14.1 us
    pallas_call x1, Pallas kernels, partial_input_of(): pl.pallas_call(input_kernel, grid=(rows // tile,), in_specs=[pl.BlockSpec...  5.67 us
    dot_general x1, matrix products, contract_rows(): lax.dot_general(left, right, (((0,), (0,)), ((), ())), preferred_element_...  5.05 us
  transfers between devices with their start and end apart: 2, of which 2 were waited for; matrix products, arithmetic and copies ran while one was open for 4% of the time, Pallas kernels for 0%

profile of v5, /device:TPU:8, one launch (start us, length us, event | category | flops | bytes accessed | tf_op | source)
XLA Modules:
  0.0 176.4 jit_solution(11920541911473960475)
XLA Ops:
  7.2 0.0 copy-start
  7.2 0.0 all-gather.2.cloned.1.call-start
  7.2 2.2 %fusion.4 = bf16[48,2304]{1,0:T(8,128)(2,1)} fusion(bf16[48,1152]{1,0:T(8,128)(2,1)} %param.11, bf16[48,1152]{1,0:T(8,128)(2,1)} %param.10, bf16[48,1152]{1,0:T(8,128)(2,1)} %param.9, pred[2304]{0:T(1024)(128)(4,1)S(1)} %iota_compare_fusion), kind=kLoop, calls=%fused_computation.9 | loop fusion | flops 2764800 | bytes 555264 | tf_op jit(solution)/shard_map/convert_element_type | solution.py:71
  9.4 0.0 all-gather.2.cloned.1.call-update
  9.4 80.9 %all-gather.2.cloned.1.call-done.both_ref = bf16[1536,2304]{1,0:T(8,128)(2,1)} async-done(((bf16[48,2304]{1,0:T(8,128)(2,1)}), bf16[1536,2304]{1,0:T(8,128)(2,1)}) %all-gather.2.cloned.1.call-update) | async-done | bytes 7077904 | tf_op jit(solution)/shard_map/all_gather | solution.py:72
  90.3 5.7 %shard_map.85 = f32[1536,256]{1,0:T(8,128)} custom-call(bf16[1536,2304]{1,0:T(8,128)(2,1)} %all-gather.2.cloned.1.call-done.both_ref, bf16[256,1152]{1,0:T(8,128)(2,1)} %gate_ref.1, bf16[256,1152]{1,0:T(8,128)(2,1)} %up_ref.1), custom_call_target="tpu_custom_call" | custom-call | flops 1811939328 | bytes 9830400 | tf_op jit(solution)/shard_map/pallas_call | solution.py:36
  95.9 14.1 %all-to-all-start = ((f32[24,64,256]{2,1,0:T(8,128)}), f32[24,64,256]{2,1,0:T(8,128)S(1)}, u32[]{:S(2)}, u32[]{:S(2)}) async-start(f32[24,64,256]{2,1,0:T(8,128)} %bitcast.5), calls=%async_computation | async-start | bytes 3145728 | tf_op jit(solution)/shard_map/all_to_all | solution.py:58
  110.1 0.0 copy-done
  110.1 5.1 %fusion = bf16[256,2304]{0,1:T(8,128)(2,1)S(1)} fusion(bf16[1536,2304]{1,0:T(8,128)(2,1)} %all-gather.2.cloned.1.call-done.both_ref, bf16[1536,256]{1,0:T(8,128)(2,1)S(1)} %copy-done), kind=kOutput, calls=%fused_computation.1 | convolution fusion | flops 1812529152 | bytes 9043968 | tf_op jit(solution)/shard_map/dot_general | solution.py:11
  115.1 0.1 fusion.10
  115.2 1.1 copy.10
  116.3 1.1 copy.9
  117.3 51.5 %all-to-all-done = f32[24,64,256]{2,1,0:T(8,128)S(1)} async-done(((f32[24,64,256]{2,1,0:T(8,128)}), f32[24,64,256]{2,1,0:T(8,128)S(1)}, u32[]{:S(2)}, u32[]{:S(2)}) %all-to-all-start) | async-done | bytes 1572896 | tf_op jit(solution)/shard_map/all_to_all | solution.py:58
  168.9 0.7 reduce_sum.9
  (1 shorter events, 0.0 us)
Async XLA Ops:
  7.2 102.9 %copy-start = (bf16[1536,256]{1,0:T(8,128)(2,1)S(1)}, bf16[1536,256]{1,0:T(8,128)(2,1)}, u32[]{:S(2)}) copy-start(bf16[1536,256]{1,0:T(8,128)(2,1)} %param.6) | copy-start | bytes 2359300
  7.2 83.1 %all-gather.2.cloned.1.call-start = ((), (), s32[]{:S(2)}) async-start(), calls=%async_computation.1 | async-start | bytes 7299072 | tf_op jit(solution)/shard_map/all_gather | solution.py:72
  95.9 72.9 %all-to-all-start = ((f32[24,64,256]{2,1,0:T(8,128)}), f32[24,64,256]{2,1,0:T(8,128)S(1)}, u32[]{:S(2)}, u32[]{:S(2)}) async-start(f32[24,64,256]{2,1,0:T(8,128)} %bitcast.5), calls=%async_computation | async-start | bytes 3145728 | tf_op jit(solution)/shard_map/all_to_all | solution.py:58
Sparse Core Ops, SparseCore 0:
  11.0 79.2 all-gather.1

commit v6 on v5

--- a/solution.py
+++ b/solution.py
@@ -2,6 +2,7 @@
 import jax.numpy as jnp
 from jax import lax
 from jax.experimental import pallas as pl
+from jax.experimental.pallas import tpu as pltpu
 from jax.sharding import PartitionSpec as P
 
 TILE_ROWS = 768
@@ -17,6 +18,29 @@
     return lax.dot_general(
         left, right, (((1,), (1,)), ((), ())), preferred_element_type=jnp.float32
     )
+
+
+def grads_kernel(gate_ref, up_ref, grad_ref, out_ref):
+    width = gate_ref.shape[1]
+    gate32 = gate_ref[...].astype(jnp.float32)
+    up32 = up_ref[...].astype(jnp.float32)
+    grad32 = grad_ref[...].astype(jnp.float32)
+    sig = jax.nn.sigmoid(gate32)
+    out_ref[:, :width] = (grad32 * up32 * sig * (1.0 + gate32 * (1.0 - sig))).astype(out_ref.dtype)
+    out_ref[:, width:] = (grad32 * gate32 * sig).astype(out_ref.dtype)
+
+
+def grads_of(gate_pre, up_pre, grad_act):
+    rows, width = gate_pre.shape
+    return pl.pallas_call(
+        grads_kernel,
+        in_specs=[pl.BlockSpec(memory_space=pltpu.VMEM)] * 3,
+        out_specs=pl.BlockSpec(memory_space=pltpu.VMEM),
+        out_shape=jax.ShapeDtypeStruct((rows, 2 * width), jnp.bfloat16),
+        cost_estimate=pl.CostEstimate(
+            flops=12 * rows * width, bytes_accessed=10 * rows * width, transcendentals=rows * width
+        ),
+    )(gate_pre, up_pre, grad_act)
 
 
 def input_kernel(both_ref, gate_ref, up_ref, out_ref):
@@ -61,15 +85,7 @@
 
 def on_device(inputs, gate_weight, up_weight, gate_pre, up_pre, grad_act):
     width = gate_pre.shape[1]
-    gate32 = jnp.concatenate([gate_pre, gate_pre], 1).astype(jnp.float32)
-    up32 = jnp.concatenate([up_pre, up_pre], 1).astype(jnp.float32)
-    grad32 = jnp.concatenate([grad_act, grad_act], 1).astype(jnp.float32)
-    sig = jax.nn.sigmoid(gate32)
-    is_gate = lax.broadcasted_iota(jnp.int32, gate32.shape, 1) < width
-    grad_both = jnp.where(
-        is_gate, grad32 * up32 * sig * (1.0 + gate32 * (1.0 - sig)), grad32 * gate32 * sig
-    ).astype(jnp.bfloat16)
-    both = lax.all_gather(grad_both, "row", axis=0, tiled=True)
+    both = lax.all_gather(grads_of(gate_pre, up_pre, grad_act), "row", axis=0, tiled=True)
     acc = contract_rows(inputs, both)
     acc_gate, acc_up = acc[:, :width], acc[:, width:]
     partial_input = partial_input_of(both, gate_weight, up_weight)

time: 177 us -> 177 us (level)
  other arithmetic: 2.87 us -> 0.71 us
  Pallas kernels: 5.67 us -> 7.54 us
    convert_element_type x1 -> x0, other arithmetic: 2.16 us -> none  [on_device(): grad_both = jnp.where(is_gate, grad32 * up32 * sig * (1.0 + gate32 * (1.0...]
    pallas_call x0 -> x1, Pallas kernels: none -> 1.87 us  [grads_of(): pl.pallas_call(grads_kernel, in_specs=[pl.BlockSpec(memory_space=pltpu.VM...]
where the time goes in v6:
time: 177 us; the launch traced here: 176 us
  waiting for transfers between devices  133 us (75%)
  starting transfers between devices  14.2 us (8%)
  between operations  14.1 us (8%)
  Pallas kernels  7.54 us (4%)
  matrix products  5.05 us (3%)
  local copies, waits for them, and re-layouts  2.2 us (1%)
    all_gather x1, waiting for transfers between devices, on_device(): lax.all_gather(grads_of(gate_pre, up_pre, grad_act), 'row', axis=0, tiled...  81.2 us
    all_to_all x1, waiting for transfers between devices, reduce_input(): pieces = lax.all_to_all(pieces, 'col', 0, 0, tiled=False)  51.5 us
    all_to_all x1, starting transfers between devices, reduce_input(): pieces = lax.all_to_all(pieces, 'col', 0, 0, tiled=False)  14.1 us
    pallas_call x1, Pallas kernels, partial_input_of(): pl.pallas_call(input_kernel, grid=(rows // tile,), in_specs=[pl.BlockSpec...  5.67 us
    dot_general x1, matrix products, contract_rows(): lax.dot_general(left, right, (((0,), (0,)), ((), ())), preferred_element_...  5.05 us
  transfers between devices with their start and end apart: 2, of which 2 were waited for; matrix products, arithmetic and copies ran while one was open for 4% of the time, Pallas kernels for 0%

profile of v6, /device:TPU:8, one launch (start us, length us, event | category | flops | bytes accessed | tf_op | source)
XLA Modules:
  0.0 176.4 jit_solution(4940418136729454778)
XLA Ops:
  7.2 0.0 copy-start
  7.2 0.0 all-gather.2.cloned.1.call-start
  7.2 1.9 %shard_map.85 = bf16[48,2304]{1,0:T(8,128)(2,1)} custom-call(bf16[48,1152]{1,0:T(8,128)(2,1)} %gate_ref.2, bf16[48,1152]{1,0:T(8,128)(2,1)} %up_ref.2, bf16[48,1152]{1,0:T(8,128)(2,1)} %grad_ref.1), custom_call_target="tpu_custom_call" | custom-call | flops 663552 | bytes 552960 | tf_op jit(solution)/shard_map/pallas_call | solution.py:35
  9.1 0.0 all-gather.2.cloned.1.call-update
  9.1 81.2 %all-gather.2.cloned.1.call-done.both_ref = bf16[1536,2304]{1,0:T(8,128)(2,1)} async-done(((bf16[48,2304]{1,0:T(8,128)(2,1)}), bf16[1536,2304]{1,0:T(8,128)(2,1)}) %all-gather.2.cloned.1.call-update) | async-done | bytes 7077904 | tf_op jit(solution)/shard_map/all_gather | solution.py:88
  90.3 5.7 %shard_map.86 = f32[1536,256]{1,0:T(8,128)} custom-call(bf16[1536,2304]{1,0:T(8,128)(2,1)} %all-gather.2.cloned.1.call-done.both_ref, bf16[256,1152]{1,0:T(8,128)(2,1)} %gate_ref.3, bf16[256,1152]{1,0:T(8,128)(2,1)} %up_ref.3), custom_call_target="tpu_custom_call" | custom-call | flops 1811939328 | bytes 9830400 | tf_op jit(solution)/shard_map/pallas_call | solution.py:60
  95.9 14.1 %all-to-all-start = ((f32[24,64,256]{2,1,0:T(8,128)}), f32[24,64,256]{2,1,0:T(8,128)S(1)}, u32[]{:S(2)}, u32[]{:S(2)}) async-start(f32[24,64,256]{2,1,0:T(8,128)} %bitcast.5), calls=%async_computation | async-start | bytes 3145728 | tf_op jit(solution)/shard_map/all_to_all | solution.py:82
  110.1 0.0 copy-done
  110.1 5.1 %fusion = bf16[256,2304]{0,1:T(8,128)(2,1)S(1)} fusion(bf16[1536,2304]{1,0:T(8,128)(2,1)} %all-gather.2.cloned.1.call-done.both_ref, bf16[1536,256]{1,0:T(8,128)(2,1)S(1)} %copy-done), kind=kOutput, calls=%fused_computation.1 | convolution fusion | flops 1812529152 | bytes 9043968 | tf_op jit(solution)/shard_map/dot_general | solution.py:12
  115.1 0.1 fusion.1
  115.2 1.1 copy.10
  116.3 1.1 copy.9
  117.3 51.5 %all-to-all-done = f32[24,64,256]{2,1,0:T(8,128)S(1)} async-done(((f32[24,64,256]{2,1,0:T(8,128)}), f32[24,64,256]{2,1,0:T(8,128)S(1)}, u32[]{:S(2)}, u32[]{:S(2)}) %all-to-all-start) | async-done | bytes 1572896 | tf_op jit(solution)/shard_map/all_to_all | solution.py:82
  168.9 0.7 reduce_sum.9
Async XLA Ops:
  7.2 102.9 %copy-start = (bf16[1536,256]{1,0:T(8,128)(2,1)S(1)}, bf16[1536,256]{1,0:T(8,128)(2,1)}, u32[]{:S(2)}) copy-start(bf16[1536,256]{1,0:T(8,128)(2,1)} %param.6) | copy-start | bytes 2359300
  7.2 83.1 %all-gather.2.cloned.1.call-start = ((), (), s32[]{:S(2)}) async-start(), calls=%async_computation.1 | async-start | bytes 7299072 | tf_op jit(solution)/shard_map/all_gather | solution.py:88
  95.9 72.9 %all-to-all-start = ((f32[24,64,256]{2,1,0:T(8,128)}), f32[24,64,256]{2,1,0:T(8,128)S(1)}, u32[]{:S(2)}, u32[]{:S(2)}) async-start(f32[24,64,256]{2,1,0:T(8,128)} %bitcast.5), calls=%async_computation | async-start | bytes 3145728 | tf_op jit(solution)/shard_map/all_to_all | solution.py:82
Sparse Core Ops, SparseCore 0:
  11.0 79.2 all-gather.1
